TPU v7x, 256 devices: a whole 4x4x8 slice. The times are simulated.
256 devices in a mesh: frame: 32 (over z, x_hi, core), head: 8 (over y, x_lo).
Axes of the slice: x: 4 (x_hi: 2, x_lo: 2; x = x_hi * 2 + x_lo), y: 4, z: 8, core: 2. Of those that a mesh axis runs over, the one named last changes fastest.
Arguments:
- query_vectors: bfloat16 [12288, 3072], P('frame', 'head'), may hold values from -17 to 17
- key_vectors: bfloat16 [12288, 3072], P('frame', 'head'), may hold values from -6 to 6
- value_vectors: bfloat16 [12288, 3072], P('frame', 'head'), may hold values from -6 to 6
- tile_mask: int32 [96, 96], replicated, may hold values from 0 to 1, as said below
- out_weight: bfloat16 [3072, 3072], P('head'), may hold values from -0.109375 to 0.109375
Outputs:
- projected: bfloat16 [12288, 3072], P(('frame', 'head'))
Inputs may be any that keep to these rules, and one draw needn't show every extreme that they name: The slab holds packed clips of whole tiles. Each clip lays its tiles out in order on a grid of latent frames by tile rows by tile columns. One clip spans 72 tiles and its latent frame holds 48 tiles, in 4 or 8 columns; every other clip has 2 to 4 rows and 2 to 4 columns, by clip. tile_mask[a, b] is 1 exactly when tiles a and b lie in the same clip and their frame, row and column indices each differ by at most 1.
All inputs are finite; a program needn't handle non-finite values.
Results may differ from a plain program's by a relative error of at most 0.02.
Values may be sent and summed in bfloat16 or wider, within the bound.
No kernel may reach another device: no remote copies, remote signals or barrier semaphores. Data moves between devices by JAX's collectives and lax.ppermute only.
A program may use at most 128 MiB of HBM per device.

v0:
```python
import math
import jax
import jax.numpy as jnp
from jax import lax
from jax.sharding import PartitionSpec as P

HD = 128
TILE = 128
NEGATIVE = -1e30


def expand_mask(tile_block, row_count, col_count):
    query_tiles, key_tiles = tile_block.shape
    tile_rows = row_count // query_tiles
    expanded = jnp.broadcast_to(
        tile_block[:, None, :, None], (query_tiles, tile_rows, key_tiles, tile_rows)
    )
    return expanded.reshape(row_count, col_count) > 0


def block_scores(query_block, key_block, allowed):
    head_count = query_block.shape[1] // HD
    query_heads = query_block.reshape(query_block.shape[0], head_count, HD)
    key_heads = key_block.reshape(key_block.shape[0], head_count, HD)
    raw_scores = jnp.einsum(
        "qhd,khd->hqk", query_heads, key_heads, preferred_element_type=jnp.float32
    ) * (1.0 / math.sqrt(HD))
    return jnp.where(allowed[None], raw_scores, NEGATIVE)


def online_update(running, key_block, value_block, allowed, query_block):
    numerator, row_top, totals = running
    scores = block_scores(query_block, key_block, allowed)
    new_top = jnp.maximum(row_top, jnp.max(scores, axis=2, keepdims=True))
    weights = jnp.where(allowed[None], jnp.exp(scores - new_top), 0.0)
    factor = jnp.exp(row_top - new_top)
    totals = totals * factor + jnp.sum(weights, axis=2, keepdims=True)
    value_heads = value_block.reshape(value_block.shape[0], row_top.shape[0], HD)
    numerator = numerator * factor + jnp.einsum(
        "hqk,khd->hqd",
        weights.astype(jnp.bfloat16),
        value_heads,
        preferred_element_type=jnp.float32,
    )
    return (numerator, new_top, totals)


def shards(query_vectors, key_vectors, value_vectors, tile_mask, out_weight):
    row_count = query_vectors.shape[0]
    channels = query_vectors.shape[1]
    head_count = channels // HD
    frame_pos = lax.axis_index("frame")
    tiles_here = row_count // TILE
    query_tiles = lax.dynamic_slice_in_dim(tile_mask, frame_pos * tiles_here, tiles_here, 0)
    initial = (
        jnp.zeros((head_count, row_count, HD), jnp.float32),
        jnp.full((head_count, row_count, 1), NEGATIVE, jnp.float32),
        jnp.zeros((head_count, row_count, 1), jnp.float32),
    )
    key_piece = lax.all_gather(key_vectors, "frame", axis=0, tiled=True)
    value_piece = lax.all_gather(value_vectors, "frame", axis=0, tiled=True)
    length = key_piece.shape[0]
    block_rows = 2 * row_count
    block_span = length // block_rows
    key_tiles = query_tiles
    key_tiles = key_tiles.reshape(tiles_here, block_span, block_rows // TILE).transpose(1, 0, 2)
    key_blocks = key_piece.reshape(block_span, block_rows, channels)
    value_blocks = value_piece.reshape(block_span, block_rows, channels)

    def advance(current, element):
        key_block, value_block, tile_block = element
        allowed = expand_mask(tile_block, row_count, block_rows)
        return (online_update(current, key_block, value_block, allowed, query_vectors), None)

    result, _ = lax.scan(advance, initial, (key_blocks, value_blocks, key_tiles))
    numerator, row_top, totals = result
    attended = (
        (numerator / totals).transpose(1, 0, 2).reshape(row_count, channels).astype(jnp.bfloat16)
    )
    return lax.psum_scatter(
        jnp.dot(attended, out_weight, preferred_element_type=jnp.float32).astype(jnp.bfloat16),
        "head",
        scatter_dimension=0,
        tiled=True,
    )


def solution(mesh):
    in_specs = (P("frame", "head"), P("frame", "head"), P("frame", "head"), P(), P("head", None))
    out_specs = P(("frame", "head"), None)
    return jax.shard_map(shards, mesh=mesh, in_specs=in_specs, out_specs=out_specs, check_vma=False)
```

profile of v0, /device:TPU:1, one launch (start us, length us, event | category | flops | bytes accessed | tf_op | source)
XLA Modules:
  0.0 568.9 jit_solution(12067339337692195843)
XLA Ops:
  11.3 107.8 %all-gather.3.cloned.1.call-done = bf16[12288,384]{1,0:T(8,128)(2,1)} async-done(((bf16[384,384]{1,0:T(8,128)(2,1)}), bf16[12288,384]{1,0:T(8,128)(2,1)}) %all-gather.3.cloned.1.call-update) | async-done | bytes 9437200 | tf_op jit(solution)/shard_map/all_gather | solution.py:60
  119.1 104.5 %all-gather.5.cloned.1.call-done = bf16[12288,384]{1,0:T(8,128)(2,1)} async-done(((bf16[384,384]{1,0:T(8,128)(2,1)}), bf16[12288,384]{1,0:T(8,128)(2,1)}) %all-gather.5.cloned.1.call-update) | async-done | bytes 9437200 | tf_op jit(solution)/shard_map/all_gather | solution.py:61
  223.6 278.3 %while.15 = (s32[]{:T(128)}, f32[3,384,128]{2,1,0:T(8,128)}, f32[3,384,1]{1,0,2:T(4,128)S(1)}, f32[3,384,1]{1,0,2:T(4,128)S(1)}, s32[16,3,6]{2,0,1:T(8,128)}, /*...) while((s32[]{:T(128)}, f32[3,384,128]{2,1,0:T(8,128)}, ...), condition=%wide.region_3.4_spmd.clone, body=%wide.region_0.3_spmd.clone.sunk | while | flops 464935680 | bytes 22782352 | solution.py:75
  228.8 3.7 fusion.33
  236.6 4.3 fusion.35
  253.8 4.5 fusion.35
  271.2 4.5 fusion.35
  288.6 4.5 fusion.35
  306.0 4.5 fusion.35
  323.4 4.5 fusion.35
  340.8 4.5 fusion.35
  358.2 4.5 fusion.35
  375.6 4.5 fusion.35
  385.3 3.7 fusion.33
  393.0 4.5 fusion.35
  410.4 4.5 fusion.35
  420.1 3.7 fusion.33
  427.8 4.5 fusion.35
  445.2 4.5 fusion.35
  462.7 4.5 fusion.35
  480.1 4.5 fusion.35
  489.7 3.7 fusion.33
  497.5 4.5 fusion.35
  506.2 56.2 %reduce-scatter.2.cloned.1.call-done = bf16[48,3072]{1,0:T(8,128)(2,1)} async-done(((bf16[384,3072]{1,0:T(8,128)(2,1)}), bf16[48,3072]{1,0:T(8,128)(2,1)}) %reduce-scatter.2.cloned.1.call-update) | async-done | bytes 294928 | tf_op jit(solution)/shard_map/reduce_scatter | solution.py:80
  (253 shorter events, 200.9 us)
Async XLA Ops:
  6.5 496.8 %copy-start = (bf16[384,3072]{1,0:T(8,128)(2,1)S(1)}, bf16[384,3072]{1,0:T(8,128)(2,1)}, u32[]{:S(2)}) copy-start(bf16[384,3072]{1,0:T(8,128)(2,1)} %param.11) | copy-start | bytes 7077892
  6.5 112.6 %all-gather.3.cloned.1.call-start = ((), (), s32[]{:S(2)}) async-start(), calls=%async_computation.1 | async-start | bytes 9732096 | tf_op jit(solution)/shard_map/all_gather | solution.py:60
  7.3 216.4 %all-gather.5.cloned.1.call-start = ((), (), s32[]{:S(2)}) async-start(), calls=%async_computation.2 | async-start | bytes 9732096 | tf_op jit(solution)/shard_map/all_gather | solution.py:61
  8.0 554.4 %reduce-scatter.2.cloned.1.call-start = ((), (), s32[]{:S(2)}) async-start(), calls=%async_computation.3 | async-start | bytes 2654208 | tf_op jit(solution)/shard_map/reduce_scatter | solution.py:80
  232.5 3.0 copy-start.1
  249.7 3.0 copy-start.1
  267.1 3.0 copy-start.1
  284.5 3.0 copy-start.1
  301.9 3.0 copy-start.1
  319.3 3.0 copy-start.1
  336.7 3.0 copy-start.1
  354.1 3.0 copy-start.1
  371.5 3.0 copy-start.1
  388.9 3.0 copy-start.1
  406.3 3.0 copy-start.1
  423.7 3.0 copy-start.1
  441.1 3.0 copy-start.1
  458.6 3.0 copy-start.1
  476.0 3.0 copy-start.1
  493.4 3.0 copy-start.1
Sparse Core Ops, SparseCore 0:
  10.1 108.9 all-gather.2
  121.9 101.6 all-gather.4
  506.3 56.0 reduce-scatter.1
where the time goes:
time: 572 us; the launch traced here: 569 us
  waiting for transfers between devices  270 us (47%)
  matrix products  132 us (23%)
  local copies, waits for them, and re-layouts  105 us (18%)
  other arithmetic  47.9 us (8%)
  between operations  13.2 us (2%)
    all_gather x1, waiting for transfers between devices, shards(): key_piece = lax.all_gather(key_vectors, 'frame', axis=0, tiled=True)  108 us
    all_gather x1, waiting for transfers between devices, shards(): value_piece = lax.all_gather(value_vectors, 'frame', axis=0, tiled=True)  104 us
    dynamic_slice x64, local copies, waits for them, and re-layouts, shards(): lax.scan(advance, initial, (key_blocks, value_blocks, key_tiles))  87.7 us
    dot_general x16, matrix products, online_update(): jnp.einsum('hqk,khd->hqd', weights.astype(jnp.bfloat16), value_heads, pre...  71.2 us
    dot_general x16, matrix products, block_scores(): jnp.einsum('qhd,khd->hqk', query_heads, key_heads, preferred_element_type...  58.4 us
    reduce_scatter x1, waiting for transfers between devices, shards(): lax.psum_scatter(jnp.dot(attended, out_weight, preferred_element_type=jnp...  56.2 us
    reduce_sum x16, other arithmetic, online_update(): totals = totals * factor + jnp.sum(weights, axis=2, keepdims=True)  47.3 us
  transfers between devices with their start and end apart: 3, of which 3 were waited for; matrix products, arithmetic and copies ran while one was open for 1% of the time, Pallas kernels for 0%

commit v1 on v0

--- a/solution.py
+++ b/solution.py
@@ -3,10 +3,17 @@
 import jax.numpy as jnp
 from jax import lax
 from jax.sharding import PartitionSpec as P
+from jax.lax import all_to_all, psum
 
 HD = 128
 TILE = 128
 NEGATIVE = -1e30
+
+
+def post_streams(in_array):
+    front = all_to_all(jnp.stack(psum(1, "frame") * [in_array]), "frame", 0, 0)
+    z = jnp.concatenate(front, axis=0)
+    return z
 
 
 def expand_mask(tile_block, row_count, col_count):
@@ -58,7 +65,7 @@
         jnp.zeros((head_count, row_count, 1), jnp.float32),
     )
     key_piece = lax.all_gather(key_vectors, "frame", axis=0, tiled=True)
-    value_piece = lax.all_gather(value_vectors, "frame", axis=0, tiled=True)
+    value_piece = post_streams(value_vectors)
     length = key_piece.shape[0]
     block_rows = 2 * row_count
     block_span = length // block_rows

time: 572 us -> 616 us (1.077)
  waiting for transfers between devices: 270 us -> 296 us
  starting transfers between devices: 0.08 us -> 12.8 us
    all_to_all x0 -> x1, waiting for transfers between devices: none -> 235 us  [post_streams(): front = all_to_all(jnp.stack(psum(1, 'frame') * [in_array]), 'frame', 0, 0)]
    all_gather x1, waiting for transfers between devices: 108 us -> 0.01 us  [shards(): key_piece = lax.all_gather(key_vectors, 'frame', axis=0, tiled=True)]
    all_gather x1 -> x0, waiting for transfers between devices: 104 us -> none  [shards(): value_piece = lax.all_gather(value_vectors, 'frame', axis=0, tiled=True)]
    all_to_all x0 -> x1, starting transfers between devices: none -> 12.8 us  [post_streams(): front = all_to_all(jnp.stack(psum(1, 'frame') * [in_array]), 'frame', 0, 0)]
    another operation x0 -> x1, local copies, waits for them, and re-layouts: none -> 6.25 us  [post_streams(): front = all_to_all(jnp.stack(psum(1, 'frame') * [in_array]), 'frame', 0, 0)]
  transfers between devices with their start and end apart: 3 -> 3, of which waited for: 3 -> 2; matrix products, arithmetic and copies ran while one was open for 1% -> 0% of each run, Pallas kernels for 0% -> 0%
where the time goes in v1:
time: 616 us; the launch traced here: 613 us
  waiting for transfers between devices  296 us (48%)
  matrix products  132 us (21%)
  local copies, waits for them, and re-layouts  110 us (18%)
  other arithmetic  47.9 us (8%)
  between operations  13.5 us (2%)
  starting transfers between devices  12.8 us (2%)
    all_to_all x1, waiting for transfers between devices, post_streams(): front = all_to_all(jnp.stack(psum(1, 'frame') * [in_array]), 'frame', 0, 0)  235 us
    dynamic_slice x64, local copies, waits for them, and re-layouts, shards(): lax.scan(advance, initial, (key_blocks, value_blocks, key_tiles))  88 us
    dot_general x16, matrix products, online_update(): jnp.einsum('hqk,khd->hqd', weights.astype(jnp.bfloat16), value_heads, pre...  70.9 us
    reduce_scatter x1, waiting for transfers between devices, shards(): lax.psum_scatter(jnp.dot(attended, out_weight, preferred_element_type=jnp...  60.7 us
    dot_general x16, matrix products, block_scores(): jnp.einsum('qhd,khd->hqk', query_heads, key_heads, preferred_element_type...  58.4 us
    reduce_sum x16, other arithmetic, online_update(): totals = totals * factor + jnp.sum(weights, axis=2, keepdims=True)  47.3 us
    all_to_all x1, starting transfers between devices, post_streams(): front = all_to_all(jnp.stack(psum(1, 'frame') * [in_array]), 'frame', 0, 0)  12.8 us
  transfers between devices with their start and end apart: 3, of which 2 were waited for; matrix products, arithmetic and copies ran while one was open for 0% of the time, Pallas kernels for 0%

profile of v1, /device:TPU:1, one launch (start us, length us, event | category | flops | bytes accessed | tf_op | source)
XLA Modules:
  0.0 613.4 jit_solution(17997110552082791891)
XLA Ops:
  6.5 6.3 %stack.2 = bf16[32,384,384]{2,1,0:T(8,128)(2,1)} broadcast(bf16[384,384]{1,0:T(8,128)(2,1)} %param.9), dimensions={1,2} | broadcast | bytes 9732096 | tf_op jit(solution)/shard_map/stack | solution.py:14
  12.8 12.8 %all-to-all-start = ((bf16[32,384,384]{2,1,0:T(8,128)(2,1)}), bf16[32,384,384]{2,1,0:T(8,128)(2,1)}, u32[]{:S(2)}, u32[]{:S(2)}) async-start(bf16[32,384,384]{2,1,0:T(8,128)(2,1)} %stack.2), calls=%async_computation | async-start | bytes 18874368 | tf_op jit(solution)/shard_map/all_to_all | solution.py:14
  28.7 234.6 %all-to-all-done = bf16[32,384,384]{2,1,0:T(8,128)(2,1)} async-done(((bf16[32,384,384]{2,1,0:T(8,128)(2,1)}), bf16[32,384,384]{2,1,0:T(8,128)(2,1)}, u32[]{:S(2)}, u32[]{:S(2)}) %all-to-all-start) | async-done | bytes 9437216 | tf_op jit(solution)/shard_map/all_to_all | solution.py:14
  263.2 278.4 %while.15 = (s32[]{:T(128)}, f32[3,384,128]{2,1,0:T(8,128)}, f32[3,384,1]{1,0,2:T(4,128)S(1)}, f32[3,384,1]{1,0,2:T(4,128)S(1)}, s32[16,3,6]{2,0,1:T(8,128)}, /*...) while((s32[]{:T(128)}, f32[3,384,128]{2,1,0:T(8,128)}, ...), condition=%wide.region_3.4_spmd.clone, body=%wide.region_0.3_spmd.clone.sunk | while | flops 464935680 | bytes 22782352 | solution.py:82
  276.2 4.3 fusion.35
  293.4 4.4 fusion.35
  310.8 4.4 fusion.35
  328.3 4.4 fusion.35
  345.7 4.4 fusion.35
  363.1 4.4 fusion.35
  380.5 4.4 fusion.35
  390.1 3.7 fusion.33
  397.9 4.4 fusion.35
  415.3 4.4 fusion.35
  432.7 4.4 fusion.35
  450.1 4.4 fusion.35
  459.8 3.7 fusion.33
  467.5 4.4 fusion.35
  484.9 4.4 fusion.35
  502.3 4.4 fusion.35
  519.7 4.4 fusion.35
  529.4 3.7 fusion.33
  537.2 4.4 fusion.35
  545.8 60.7 %reduce-scatter.2.cloned.1.call-done = bf16[48,3072]{1,0:T(8,128)(2,1)} async-done(((bf16[384,3072]{1,0:T(8,128)(2,1)}), bf16[48,3072]{1,0:T(8,128)(2,1)}) %reduce-scatter.2.cloned.1.call-update) | async-done | bytes 294928 | tf_op jit(solution)/shard_map/reduce_scatter | solution.py:87
  (255 shorter events, 203.2 us)
Async XLA Ops:
  6.5 536.4 %copy-start = (bf16[384,3072]{1,0:T(8,128)(2,1)S(1)}, bf16[384,3072]{1,0:T(8,128)(2,1)}, u32[]{:S(2)}) copy-start(bf16[384,3072]{1,0:T(8,128)(2,1)} %param.11) | copy-start | bytes 7077892
  12.8 15.0 %copy-start.2 = (bf16[384,384]{1,0:T(8,128)(2,1)S(1)}, bf16[384,384]{1,0:T(8,128)(2,1)}, u32[]{:S(2)}) copy-start(bf16[384,384]{1,0:T(8,128)(2,1)} %param.7) | copy-start | bytes 884740
  12.8 250.4 %all-to-all-start = ((bf16[32,384,384]{2,1,0:T(8,128)(2,1)}), bf16[32,384,384]{2,1,0:T(8,128)(2,1)}, u32[]{:S(2)}, u32[]{:S(2)}) async-start(bf16[32,384,384]{2,1,0:T(8,128)(2,1)} %stack.2), calls=%async_computation | async-start | bytes 18874368 | tf_op jit(solution)/shard_map/all_to_all | solution.py:14
  25.6 237.7 %all-gather.2.cloned.1.call-start = ((), (), s32[]{:S(2)}) async-start(), calls=%async_computation.2 | async-start | bytes 9732096 | tf_op jit(solution)/shard_map/all_gather | solution.py:67
  26.3 580.2 %reduce-scatter.2.cloned.1.call-start = ((), (), s32[]{:S(2)}) async-start(), calls=%async_computation.3 | async-start | bytes 2654208 | tf_op jit(solution)/shard_map/reduce_scatter | solution.py:87
  272.1 3.0 copy-start.1
  289.3 3.0 copy-start.1
  306.8 3.0 copy-start.1
  324.2 3.0 copy-start.1
  341.6 3.0 copy-start.1
  359.0 3.0 copy-start.1
  376.4 3.0 copy-start.1
  393.8 3.0 copy-start.1
  411.2 3.0 copy-start.1
  428.6 3.0 copy-start.1
  446.0 3.0 copy-start.1
  463.4 3.0 copy-start.1
  480.8 3.0 copy-start.1
  498.2 3.0 copy-start.1
  515.7 3.0 copy-start.1
  533.1 3.0 copy-start.1
Sparse Core Ops, SparseCore 0:
  29.1 180.5 all-gather.1
  545.9 60.5 reduce-scatter.1
